TPU v7x, 256 devices: a whole 4x4x8 slice. The times are simulated.
256 devices in a mesh: dp: 4 (over y), expert: 64 (over z, x, core).
Axes of the slice: x: 4, y: 4, z: 8, core: 2. Of those that a mesh axis runs over, the one named last changes fastest.
Arguments:
- hidden_states: bfloat16 [1024, 4, 4096], P('expert'), may hold values from -6 to 6
- routes: int32 [1024, 4, 8], P('expert'), may hold values from 0 to 63, all different within a row; in each aligned block of 64 rows (0 to 63, 64 to 127, ..., all dimensions but the last counted through in order) at most 16 rows name the same one
- route_weight: float32 [1024, 4, 8], P('expert'), may hold values from 0.05 to 1
- finish_step: int32 [1024], P('expert'), may hold values from 1 to 4
- group_keep: int32 [64], P('expert'), may hold values from 0 to 1
- dest_slot: int32 [1024], P('expert'), may hold values from 0 to 1023, as said below
- w_gate: bfloat16 [64, 4096, 1536], P('expert', None, 'dp'), may hold values from -0.09375 to 0.09375
- w_up: bfloat16 [64, 4096, 1536], P('expert', None, 'dp'), may hold values from -0.09375 to 0.09375
- w_down: bfloat16 [64, 1536, 4096], P('expert', 'dp'), may hold values from -0.15625 to 0.15625
Outputs:
- trainer_rows: bfloat16 [1024, 4, 4096], P(('dp', 'expert'))
Inputs may be any that keep to these rules, and one draw needn't show every extreme that they name: `routes`: in the 64 row-steps of one prompt group (rows g * 16 to (g + 1) * 16 - 1, all steps), no expert is named more than 16 times, a bound that some block reaches; a row names 8 different experts at each step. dest_slot is a permutation of the slots; row r of group g = r // 16 goes to a slot (d * 64 + g) * 4 + i with 0 <= d < 4 and 0 <= i < 4.
All inputs are finite; a program needn't handle non-finite values.
Results may differ from a plain program's by a relative error of at most 0.0049.
Values may be sent and summed in bfloat16 or wider, within the bound.
No kernel may reach another device: no remote copies, remote signals or barrier semaphores. Data moves between devices by JAX's collectives and lax.ppermute only.
A program may use at most 128 MiB of HBM per device.

v0:
```python
import jax
import jax.numpy as jnp
from jax import lax
from jax.sharding import PartitionSpec as P

MOST_BASE = 16


def exchange_gather(matrix, replica, replica_count):
    width = matrix.shape[1] // replica_count
    pieces = [lax.dynamic_slice_in_dim(matrix, replica * width, width, axis=1)]
    for shift in range(1, replica_count):
        start = (replica + shift) % replica_count * width
        outgoing = lax.dynamic_slice_in_dim(matrix, start, width, axis=1)
        pairs = [(i, (i + shift) % replica_count) for i in range(replica_count)]
        pieces.append(lax.ppermute(outgoing, "dp", pairs))
    return pieces


def exchange_all(block, replica_count):
    pieces = [block]
    for shift in range(1, replica_count):
        pairs = [(i, (i + shift) % replica_count) for i in range(replica_count)]
        pieces.append(lax.ppermute(block, "dp", pairs))
    return jnp.stack(pieces, axis=0)


def body(
    hidden_states, routes, route_weight, finish_step, group_keep, dest_slot, w_gate, w_up, w_down
):
    expert_count = lax.axis_size("expert")
    replica_count = lax.axis_size("dp")
    replica = lax.axis_index("dp")
    row_count, step_count, model_width = hidden_states.shape
    top_count = routes.shape[2]
    hidden_part = w_down.shape[1]
    columns = model_width // replica_count
    tokens = row_count * step_count
    slot_count = min(tokens, max(MOST_BASE, 2 * tokens * top_count // expert_count))
    slot_count = -(-slot_count // replica_count) * replica_count
    part = slot_count // replica_count
    down_cols = exchange_gather(w_down[0], replica, replica_count)
    step_ids = lax.broadcasted_iota(jnp.int32, (row_count, step_count), 1)
    live_mask = ((step_ids < finish_step[:, None]) & (group_keep[0] == 1)).reshape(tokens)
    gate_share = route_weight / jnp.sum(route_weight, axis=2, keepdims=True)
    expert_ids = lax.broadcasted_iota(jnp.int32, (1, 1, expert_count), 2)
    picked = (routes.reshape(tokens, top_count, 1) == expert_ids) & live_mask[:, None, None]
    hit_mask = jnp.sum(picked.astype(jnp.int32), axis=1)
    share_wide = jnp.broadcast_to(gate_share.reshape(tokens, top_count, 1), picked.shape)
    weight = jnp.sum(jnp.where(picked, share_wide, jnp.zeros_like(share_wide)), axis=1)
    prior_hits = jnp.cumsum(hit_mask, axis=0) - hit_mask
    flat_inputs = hidden_states.reshape(tokens, model_width)
    chunks = 2 if part % 2 == 0 else 1
    sub = part // chunks
    member_ids = lax.broadcasted_iota(jnp.int32, (1, 1, replica_count, 1), 2)
    within_ids = lax.broadcasted_iota(jnp.int32, (1, 1, 1, sub), 3)
    combined = jnp.zeros((tokens, columns), jnp.float32)
    outgoings = []
    for chunk in range(chunks):
        slot_ids = replica * part + chunk * sub + lax.broadcasted_iota(jnp.int32, (1, 1, sub), 2)
        placement = (hit_mask[:, :, None] == 1) & (prior_hits[:, :, None] == slot_ids)
        placement = placement.reshape(tokens, expert_count * sub)
        outgoings.append(
            lax.dot_general(
                placement.astype(jnp.bfloat16),
                flat_inputs,
                (((0,), (0,)), ((), ())),
                preferred_element_type=jnp.float32,
            ).astype(jnp.bfloat16)
        )
    if chunks > 1:
        down_cols, outgoings[1] = lax.optimization_barrier((down_cols, outgoings[1]))
    down_stack = jnp.stack(down_cols, axis=0)
    for chunk in range(chunks):
        outgoing = outgoings[chunk]
        arrived = lax.all_to_all(outgoing, "expert", split_axis=0, concat_axis=0, tiled=True)
        gathered = lax.all_gather(arrived, "dp", axis=0, tiled=True)
        gate_part = jnp.dot(gathered, w_gate[0], preferred_element_type=jnp.float32)
        up_part = jnp.dot(gathered, w_up[0], preferred_element_type=jnp.float32)
        activated = (jax.nn.silu(gate_part) * up_part).astype(jnp.bfloat16)
        hidden_all = exchange_all(activated, replica_count)
        expert_cols = lax.dot_general(
            hidden_all, down_stack, (((0, 2), (0, 1)), ((), ())), preferred_element_type=jnp.float32
        ).astype(jnp.bfloat16)
        by_source = expert_cols.reshape(replica_count, expert_count, sub, columns).transpose(
            1, 0, 2, 3
        )
        returned_rows = lax.all_to_all(by_source, "expert", split_axis=0, concat_axis=0, tiled=True)
        all_slot_ids = member_ids * part + chunk * sub + within_ids
        weighted_place = jnp.where(
            (hit_mask[:, :, None, None] == 1) & (prior_hits[:, :, None, None] == all_slot_ids),
            weight[:, :, None, None],
            0.0,
        ).reshape(tokens, expert_count * replica_count * sub)
        combined = combined + jnp.dot(
            weighted_place,
            returned_rows.reshape(expert_count * replica_count * sub, columns).astype(jnp.float32),
            precision=lax.Precision.HIGH,
            preferred_element_type=jnp.float32,
        )
    share_rows = row_count // replica_count
    flat_device = dest_slot // share_rows
    target = flat_device // expert_count * share_rows + dest_slot % share_rows
    position_ids = lax.broadcasted_iota(jnp.int32, (replica_count * share_rows, row_count), 0)
    arrangement = (target[None, :] == position_ids).astype(jnp.bfloat16)
    arranged = jnp.dot(
        arrangement,
        combined.astype(jnp.bfloat16).reshape(row_count, step_count * columns),
        preferred_element_type=jnp.float32,
    ).astype(jnp.bfloat16)
    arranged = arranged.reshape(replica_count, share_rows, step_count, columns)
    quarters = lax.all_to_all(arranged, "dp", split_axis=0, concat_axis=0, tiled=True)
    return quarters.transpose(1, 2, 0, 3).reshape(share_rows, step_count, model_width)


def solution(mesh):
    in_specs = (
        P("expert", None, None),
        P("expert", None, None),
        P("expert", None, None),
        P("expert"),
        P("expert"),
        P("expert"),
        P("expert", None, "dp"),
        P("expert", None, "dp"),
        P("expert", "dp", None),
    )
    out_specs = P(("dp", "expert"), None, None)
    return jax.shard_map(body, mesh=mesh, in_specs=in_specs, out_specs=out_specs, check_vma=False)
```

profile of v0, /device:TPU:2, one launch (start us, length us, event | category | flops | bytes accessed | tf_op | source)
XLA Modules:
  0.0 302.3 jit_solution(9261390843322471953)
XLA Ops:
  6.5 3.7 %dynamic-slice_bitcast_fusion = (bf16[384,1024]{1,0:T(8,128)(2,1)}, bf16[384,1024]{1,0:T(8,128)(2,1)}, bf16[384,1024]{1,0:T(8,128)(2,1)}, bf16[384,1024]{1,0:T(8,128)(2,1)}) fusion(bf16[1,384,4096]{2,1,0:T(8,128)(2,1)} %param.17, s32[]{:T(128)S(6)} %select_n.63, s32[]{:T(128)S(6)} %select_n.59, s32[]{:T(128)S(6)} %select_n.57, s32[]{:T(128)S(6)} %select_n.61), kind=kLoop, calls=%fused_computation.40 | loop fusion | bytes 6291472 | tf_op jit(solution)/shard_map/dynamic_slice | solution.py:14
  11.9 2.9 collective-permute-start.4
  22.2 9.0 %collective-permute-done.3 = bf16[384,1024]{1,0:T(8,128)(2,1)} collective-permute-done((bf16[384,1024]{1,0:T(8,128)(2,1)}, bf16[384,1024]{1,0:T(8,128)(2,1)}, u32[]{:S(2)}, u32[]{:S(2)}) %collective-permute-start.3) | collective-permute-done | bytes 786464 | tf_op jit(solution)/shard_map/ppermute | solution.py:16
  31.2 18.0 %collective-permute-done.4 = bf16[384,1024]{1,0:T(8,128)(2,1)} collective-permute-done((bf16[384,1024]{1,0:T(8,128)(2,1)}, bf16[384,1024]{1,0:T(8,128)(2,1)}, u32[]{:S(2)}, u32[]{:S(2)}) %collective-permute-start.4) | collective-permute-done | bytes 786464 | tf_op jit(solution)/shard_map/ppermute | solution.py:16
  51.7 40.9 %all_to_all.39 = bf16[64,2,4096]{2,1,0:T(2,128)(2,1)} all-to-all(bf16[64,2,4096]{2,1,0:T(2,128)(2,1)} %all_to_all.29), channel_id=1, replica_groups=mesh['dp'=4,'expert'=64] {'expert'}, dimensions={0} | all-to-all | bytes 2097152 | tf_op jit(solution)/shard_map/all_to_all | solution.py:76
  100.1 34.6 %all_to_all.40 = bf16[64,2,4096]{2,1,0:T(2,128)(2,1)} all-to-all(bf16[64,2,4096]{2,1,0:T(2,128)(2,1)} %all_to_all.25), channel_id=1, replica_groups=mesh['dp'=4,'expert'=64] {'expert'}, dimensions={0} | all-to-all | bytes 2097152 | tf_op jit(solution)/shard_map/all_to_all | solution.py:76
  136.9 5.0 %all-gather.5.cloned.1.call-done = bf16[512,4096]{1,0:T(8,128)(2,1)} async-done(((bf16[128,4096]{1,0:T(8,128)(2,1)}), bf16[512,4096]{1,0:T(8,128)(2,1)}) %all-gather.5.cloned.1.call-update) | async-done | bytes 4194320 | tf_op jit(solution)/shard_map/all_gather | solution.py:77
  142.0 4.7 %fusion.4 = f32[512,384]{1,0:T(8,128)S(1)} fusion(bf16[512,4096]{1,0:T(8,128)(2,1)} %all-gather.5.cloned.1.call-done, bf16[1,4096,384]{2,1,0:T(8,128)(2,1)S(1)} %copy-done), kind=kOutput, calls=%fused_computation.8 | convolution fusion | flops 1610612736 | bytes 8126464 | tf_op jit(solution)/shard_map/dot_general | solution.py:78
  152.6 9.2 %collective-permute-done.8 = bf16[512,384]{1,0:T(8,128)(2,1)S(1)} collective-permute-done((bf16[512,384]{1,0:T(8,128)(2,1)S(1)}, bf16[512,384]{1,0:T(8,128)(2,1)S(1)}, u32[]{:S(2)}, u32[]{:S(2)}) %collective-permute-start.8) | collective-permute-done | bytes 393248 | tf_op jit(solution)/shard_map/ppermute | solution.py:24
  161.8 4.5 %collective-permute-done.7 = bf16[512,384]{1,0:T(8,128)(2,1)S(1)} collective-permute-done((bf16[512,384]{1,0:T(8,128)(2,1)S(1)}, bf16[512,384]{1,0:T(8,128)(2,1)S(1)}, u32[]{:S(2)}, u32[]{:S(2)}) %collective-permute-start.7) | collective-permute-done | bytes 393248 | tf_op jit(solution)/shard_map/ppermute | solution.py:24
  166.3 14.4 %collective-permute-done.6 = bf16[512,384]{1,0:T(8,128)(2,1)S(1)} collective-permute-done((bf16[512,384]{1,0:T(8,128)(2,1)S(1)}, bf16[512,384]{1,0:T(8,128)(2,1)S(1)}, u32[]{:S(2)}, u32[]{:S(2)}) %collective-permute-start.6) | collective-permute-done | bytes 393248 | tf_op jit(solution)/shard_map/ppermute | solution.py:24
  180.7 4.5 %bitcast_convert_fusion = bf16[512,1024]{1,0:T(8,128)(2,1)} fusion(bf16[1,512,384]{2,1,0:T(8,128)(2,1)S(1)} %bitcast.91, bf16[1,512,384]{2,1,0:T(8,128)(2,1)S(1)} %bitcast.93, bf16[1,512,384]{2,1,0:T(8,128)(2,1)S(1)} %bitcast.94, bf16[1,512,384]{2,1,0:T(8,128)(2,1)S(1)} %bitcast.88, bf16[1,384,1024]{2,1,0:T(8,128)(2,1)} %bitcast.16, ...), kind=kOutput, calls=%fused_computation.12 | convolution fusion | flops 1618214912 | bytes 5767168 | tf_op jit(solution)/shard_map/dot_general | solution.py:82
  187.5 3.4 %copy.47 = bf16[4,64,2,1024]{3,2,0,1:T(2,128)(2,1)} copy(bf16[4,64,2,1024]{3,2,1,0:T(2,128)(2,1)} %reshape.215) | data formatting | bytes 2097152 | tf_op jit(solution)/shard_map/reshape | solution.py:85
  190.8 10.7 %all-to-all-start.3 = ((bf16[64,4,2,1024]{3,2,1,0:T(2,128)(2,1)}), bf16[64,4,2,1024]{3,2,1,0:T(2,128)(2,1)}, u32[]{:S(2)}, u32[]{:S(2)}) async-start(bf16[64,4,2,1024]{3,2,1,0:T(2,128)(2,1)} %bitcast.79), calls=%async_computation.3 | async-start | bytes 2097152 | tf_op jit(solution)/shard_map/all_to_all | solution.py:88
  201.6 3.2 %all-gather.3.cloned.1.call-done = bf16[512,4096]{1,0:T(8,128)(2,1)} async-done(((bf16[128,4096]{1,0:T(8,128)(2,1)}), bf16[512,4096]{1,0:T(8,128)(2,1)}) %all-gather.3.cloned.1.call-update) | async-done | bytes 4194320 | tf_op jit(solution)/shard_map/all_gather | solution.py:77
  204.8 4.7 %fusion.6 = f32[512,384]{1,0:T(8,128)S(1)} fusion(bf16[512,4096]{1,0:T(8,128)(2,1)} %all-gather.3.cloned.1.call-done, bf16[1,4096,384]{2,1,0:T(8,128)(2,1)S(1)} %copy-done), kind=kOutput, calls=%fused_computation.10 | convolution fusion | flops 1610612736 | bytes 8126464 | tf_op jit(solution)/shard_map/dot_general | solution.py:78
  215.1 8.8 %collective-permute-done.2 = bf16[512,384]{1,0:T(8,128)(2,1)S(1)} collective-permute-done((bf16[512,384]{1,0:T(8,128)(2,1)S(1)}, bf16[512,384]{1,0:T(8,128)(2,1)S(1)}, u32[]{:S(2)}, u32[]{:S(2)}) %collective-permute-start.2) | collective-permute-done | bytes 393248 | tf_op jit(solution)/shard_map/ppermute | solution.py:24
  226.1 7.2 %collective-permute-done = bf16[512,384]{1,0:T(8,128)(2,1)S(1)} collective-permute-done((bf16[512,384]{1,0:T(8,128)(2,1)S(1)}, bf16[512,384]{1,0:T(8,128)(2,1)S(1)}, u32[]{:S(2)}, u32[]{:S(2)}) %collective-permute-start) | collective-permute-done | bytes 393248 | tf_op jit(solution)/shard_map/ppermute | solution.py:24
  233.3 4.4 %bitcast_convert_fusion.1 = bf16[512,1024]{1,0:T(8,128)(2,1)} fusion(bf16[1,512,384]{2,1,0:T(8,128)(2,1)S(1)} %bitcast.89, bf16[1,512,384]{2,1,0:T(8,128)(2,1)S(1)} %bitcast.90, bf16[1,512,384]{2,1,0:T(8,128)(2,1)S(1)} %bitcast.92, bf16[1,512,384]{2,1,0:T(8,128)(2,1)S(1)} %bitcast.87, bf16[1,384,1024]{2,1,0:T(8,128)(2,1)} %bitcast.16, ...), kind=kOutput, calls=%fused_computation.13 | convolution fusion | flops 1618214912 | bytes 5767168 | tf_op jit(solution)/shard_map/dot_general | solution.py:82
  239.9 3.4 %copy.48 = bf16[4,64,2,1024]{3,2,0,1:T(2,128)(2,1)} copy(bf16[4,64,2,1024]{3,2,1,0:T(2,128)(2,1)} %reshape.214) | data formatting | bytes 2097152 | tf_op jit(solution)/shard_map/reshape | solution.py:85
  243.3 10.7 %all-to-all-start.1 = ((bf16[64,4,2,1024]{3,2,1,0:T(2,128)(2,1)}), bf16[64,4,2,1024]{3,2,1,0:T(2,128)(2,1)}, u32[]{:S(2)}, u32[]{:S(2)}) async-start(bf16[64,4,2,1024]{3,2,1,0:T(2,128)(2,1)} %bitcast.80), calls=%async_computation.1 | async-start | bytes 2097152 | tf_op jit(solution)/shard_map/all_to_all | solution.py:88
  254.7 3.5 %convolution_bitcast_fusion = f32[64,1024]{1,0:T(8,128)} fusion(bf16[64,4,2,1024]{3,2,1,0:T(2,128)(2,1)} %all-to-all-done.3, s32[4,2]{1,0:T(4,128)S(1)} %iota_add_fusion, f32[64,64]{1,0:T(8,128)S(1)} %select_reduce_fusion, s32[64,64]{1,0:T(8,128)S(1)} %sub.20, pred[64,64]{1,0:T(8,128)(4,1)S(1)} %broadcast_compare_fusion), kind=kOutput, calls=%fused_computation.32 | convolution fusion | flops 201424896 | bytes 1347616 | tf_op jit(solution)/shard_map/dot_general | solution.py:95
  258.2 24.6 %all-to-all-done.1 = bf16[64,4,2,1024]{3,2,1,0:T(2,128)(2,1)} async-done(((bf16[64,4,2,1024]{3,2,1,0:T(2,128)(2,1)}), bf16[64,4,2,1024]{3,2,1,0:T(2,128)(2,1)}, u32[]{:S(2)}, u32[]{:S(2)}) %all-to-all-start.1) | async-done | bytes 1048608 | tf_op jit(solution)/shard_map/all_to_all | solution.py:88
  285.9 8.8 %all_to_all.41 = bf16[4,4,4,1024]{3,2,1,0:T(4,128)(2,1)S(1)} all-to-all(bf16[4,4,4,1024]{3,2,1,0:T(4,128)(2,1)S(1)} %reshape.217), channel_id=1, replica_groups=mesh['dp'=4,'expert'=64] {'dp'}, dimensions={0} | all-to-all | bytes 262144 | tf_op jit(solution)/shard_map/all_to_all | solution.py:112
  (75 shorter events, 43.2 us)
Async XLA Ops:
  6.5 135.4 %copy-start = (bf16[1,4096,384]{2,1,0:T(8,128)(2,1)S(1)}, bf16[1,4096,384]{2,1,0:T(8,128)(2,1)}, u32[]{:S(2)}) copy-start(bf16[1,4096,384]{2,1,0:T(8,128)(2,1)} %param.15) | copy-start | bytes 9437188
  6.5 135.4 %all-gather.5.cloned.1.call-start = ((), (), s32[]{:S(2)}) async-start(), calls=%async_computation.6 | async-start | bytes 5242880 | tf_op jit(solution)/shard_map/all_gather | solution.py:77
  6.5 9.6 %copy-start.4 = (s32[16,4,8]{0,2,1:T(8,128)S(1)}, s32[16,4,8]{0,2,1:T(8,128)}, u32[]{:S(2)}) copy-start(s32[16,4,8]{0,2,1:T(8,128)} %param.10) | copy-start | bytes 6148
  6.5 10.3 %copy-start.5 = (s32[16]{0:T(128)S(1)}, s32[16]{0:T(128)}, u32[]{:S(2)}) copy-start(s32[16]{0:T(128)} %param.12) | copy-start | bytes 196
  10.3 20.9 %collective-permute-start.3 = (bf16[384,1024]{1,0:T(8,128)(2,1)}, bf16[384,1024]{1,0:T(8,128)(2,1)}, u32[]{:S(2)}, u32[]{:S(2)}) collective-permute-start(bf16[384,1024]{1,0:T(8,128)(2,1)} %get-tuple-element.16), channel_id=1, source_target_pairs={{0,64},{64,128},{128,192},{192,0},{1,65},{65,129},{129,193},{193,1... | collective-permute-start | bytes 2359304 | tf_op jit(solution)/shard_map/ppermute | solution.py:16
  11.9 37.3 %collective-permute-start.4 = (bf16[384,1024]{1,0:T(8,128)(2,1)}, bf16[384,1024]{1,0:T(8,128)(2,1)}, u32[]{:S(2)}, u32[]{:S(2)}) collective-permute-start(bf16[384,1024]{1,0:T(8,128)(2,1)} %get-tuple-element.18), channel_id=1, source_target_pairs={{0,128},{64,192},{128,0},{192,64},{1,129},{65,193},{129,1},{193,65... | collective-permute-start | bytes 2359304 | tf_op jit(solution)/shard_map/ppermute | solution.py:16
  14.8 34.4 %collective-permute-start.5 = (bf16[384,1024]{1,0:T(8,128)(2,1)}, bf16[384,1024]{1,0:T(8,128)(2,1)}, u32[]{:S(2)}, u32[]{:S(2)}) collective-permute-start(bf16[384,1024]{1,0:T(8,128)(2,1)} %get-tuple-element.15), channel_id=1, source_target_pairs={{0,192},{64,0},{128,64},{192,128},{1,193},{65,1},{129,65},{193,129... | collective-permute-start | bytes 2359304 | tf_op jit(solution)/shard_map/ppermute | solution.py:16
  95.0 109.8 %all-gather.3.cloned.1.call-start = ((), (), s32[]{:S(2)}) async-start(), calls=%async_computation.5 | async-start | bytes 5242880 | tf_op jit(solution)/shard_map/all_gather | solution.py:77
  142.0 4.7 %copy-start.7 = (bf16[512,4096]{1,0:T(8,128)(2,1)S(1)}, bf16[512,4096]{1,0:T(8,128)(2,1)}, u32[]{:S(2)}) copy-start(bf16[512,4096]{1,0:T(8,128)(2,1)} %all-gather.5.cloned.1.call-done) | copy-start | bytes 12582916
  142.0 4.7 %copy-start.8 = (bf16[1,4096,384]{2,1,0:T(8,128)(2,1)S(1)}, bf16[1,4096,384]{2,1,0:T(8,128)(2,1)}, u32[]{:S(2)}) copy-start(bf16[1,4096,384]{2,1,0:T(8,128)(2,1)} %param.16) | copy-start | bytes 9437188
  146.6 34.1 %copy-start.1 = (bf16[384,1024]{1,0:T(8,128)(2,1)S(1)}, bf16[384,1024]{1,0:T(8,128)(2,1)}, u32[]{:S(2)}) copy-start(bf16[384,1024]{1,0:T(8,128)(2,1)} %get-tuple-element.10) | copy-start | bytes 2359300
  149.0 12.8 %collective-permute-start.8 = (bf16[512,384]{1,0:T(8,128)(2,1)S(1)}, bf16[512,384]{1,0:T(8,128)(2,1)S(1)}, u32[]{:S(2)}, u32[]{:S(2)}) collective-permute-start(bf16[512,384]{1,0:T(8,128)(2,1)S(1)} %fusion.28), channel_id=1, source_target_pairs={{0,192},{64,0},{128,64},{192,128},{1,193},{65,1},{129,65},{193,129... | collective-permute-start | bytes 1179656 | tf_op jit(solution)/shard_map/ppermute | solution.py:24
  150.2 16.1 %collective-permute-start.7 = (bf16[512,384]{1,0:T(8,128)(2,1)S(1)}, bf16[512,384]{1,0:T(8,128)(2,1)S(1)}, u32[]{:S(2)}, u32[]{:S(2)}) collective-permute-start(bf16[512,384]{1,0:T(8,128)(2,1)S(1)} %fusion.28), channel_id=1, source_target_pairs={{0,128},{64,192},{128,0},{192,64},{1,129},{65,193},{129,1},{193,65... | collective-permute-start | bytes 1179656 | tf_op jit(solution)/shard_map/ppermute | solution.py:24
  152.0 28.7 %collective-permute-start.6 = (bf16[512,384]{1,0:T(8,128)(2,1)S(1)}, bf16[512,384]{1,0:T(8,128)(2,1)S(1)}, u32[]{:S(2)}, u32[]{:S(2)}) collective-permute-start(bf16[512,384]{1,0:T(8,128)(2,1)S(1)} %fusion.28), channel_id=1, source_target_pairs={{0,64},{64,128},{128,192},{192,0},{1,65},{65,129},{129,193},{193,1... | collective-permute-start | bytes 1179656 | tf_op jit(solution)/shard_map/ppermute | solution.py:24
  190.8 52.5 %all-to-all-start.3 = ((bf16[64,4,2,1024]{3,2,1,0:T(2,128)(2,1)}), bf16[64,4,2,1024]{3,2,1,0:T(2,128)(2,1)}, u32[]{:S(2)}, u32[]{:S(2)}) async-start(bf16[64,4,2,1024]{3,2,1,0:T(2,128)(2,1)} %bitcast.79), calls=%async_computation.3 | async-start | bytes 2097152 | tf_op jit(solution)/shard_map/all_to_all | solution.py:88
  204.8 4.7 %copy-start.6 = (bf16[512,4096]{1,0:T(8,128)(2,1)S(1)}, bf16[512,4096]{1,0:T(8,128)(2,1)}, u32[]{:S(2)}) copy-start(bf16[512,4096]{1,0:T(8,128)(2,1)} %all-gather.3.cloned.1.call-done) | copy-start | bytes 12582916
  204.8 4.7 %copy-start.9 = (bf16[1,4096,384]{2,1,0:T(8,128)(2,1)S(1)}, bf16[1,4096,384]{2,1,0:T(8,128)(2,1)}, u32[]{:S(2)}) copy-start(bf16[1,4096,384]{2,1,0:T(8,128)(2,1)} %param.16) | copy-start | bytes 9437188
  209.5 23.8 %copy-start.2 = (bf16[384,1024]{1,0:T(8,128)(2,1)S(1)}, bf16[384,1024]{1,0:T(8,128)(2,1)}, u32[]{:S(2)}) copy-start(bf16[384,1024]{1,0:T(8,128)(2,1)} %get-tuple-element.10) | copy-start | bytes 2359300
  211.8 12.0 %collective-permute-start.2 = (bf16[512,384]{1,0:T(8,128)(2,1)S(1)}, bf16[512,384]{1,0:T(8,128)(2,1)S(1)}, u32[]{:S(2)}, u32[]{:S(2)}) collective-permute-start(bf16[512,384]{1,0:T(8,128)(2,1)S(1)} %fusion.31), channel_id=1, source_target_pairs={{0,192},{64,0},{128,64},{192,128},{1,193},{65,1},{129,65},{193,129... | collective-permute-start | bytes 1179656 | tf_op jit(solution)/shard_map/ppermute | solution.py:24
  212.5 13.6 %collective-permute-start.1 = (bf16[512,384]{1,0:T(8,128)(2,1)S(1)}, bf16[512,384]{1,0:T(8,128)(2,1)S(1)}, u32[]{:S(2)}, u32[]{:S(2)}) collective-permute-start(bf16[512,384]{1,0:T(8,128)(2,1)S(1)} %fusion.31), channel_id=1, source_target_pairs={{0,128},{64,192},{128,0},{192,64},{1,129},{65,193},{129,1},{193,65... | collective-permute-start | bytes 1179656 | tf_op jit(solution)/shard_map/ppermute | solution.py:24
  214.3 18.9 %collective-permute-start = (bf16[512,384]{1,0:T(8,128)(2,1)S(1)}, bf16[512,384]{1,0:T(8,128)(2,1)S(1)}, u32[]{:S(2)}, u32[]{:S(2)}) collective-permute-start(bf16[512,384]{1,0:T(8,128)(2,1)S(1)} %fusion.31), channel_id=1, source_target_pairs={{0,64},{64,128},{128,192},{192,0},{1,65},{65,129},{129,193},{193,1... | collective-permute-start | bytes 1179656 | tf_op jit(solution)/shard_map/ppermute | solution.py:24
  237.7 16.4 %copy-start.3 = (f32[16,4,8]{0,2,1:T(8,128)S(1)}, f32[16,4,8]{0,2,1:T(8,128)}, u32[]{:S(2)}) copy-start(f32[16,4,8]{0,2,1:T(8,128)} %param.11) | copy-start | bytes 6148
  237.7 16.8 %copy-start.10 = (s32[16]{0:T(128)S(1)}, s32[16]{0:T(128)}, u32[]{:S(2)}) copy-start(s32[16]{0:T(128)} %param.14) | copy-start | bytes 196
  243.3 39.5 %all-to-all-start.1 = ((bf16[64,4,2,1024]{3,2,1,0:T(2,128)(2,1)}), bf16[64,4,2,1024]{3,2,1,0:T(2,128)(2,1)}, u32[]{:S(2)}, u32[]{:S(2)}) async-start(bf16[64,4,2,1024]{3,2,1,0:T(2,128)(2,1)} %bitcast.80), calls=%async_computation.1 | async-start | bytes 2097152 | tf_op jit(solution)/shard_map/all_to_all | solution.py:88
Sparse Core Ops, SparseCore 0:
  95.1 46.8 all-gather.4
  143.8 60.9 all-gather.2
where the time goes:
time: 303 us; the launch traced here: 302 us
  waiting for transfers between devices  106 us (35%)
  blocking collectives  84.3 us (28%)
  matrix products  34.3 us (11%)
  starting transfers between devices  34.2 us (11%)
  local copies, waits for them, and re-layouts  28 us (9%)
  between operations  14.3 us (5%)
    all_to_all x2, blocking collectives, body(): lax.all_to_all(outgoing, 'expert', split_axis=0, concat_axis=0, tiled=True)  75.5 us
    ppermute x6, waiting for transfers between devices, exchange_all(): pieces.append(lax.ppermute(block, 'dp', pairs))  46.3 us
    ppermute x3, waiting for transfers between devices, exchange_gather(): pieces.append(lax.ppermute(outgoing, 'dp', pairs))  27 us
    all_to_all x2, waiting for transfers between devices, body(): lax.all_to_all(by_source, 'expert', split_axis=0, concat_axis=0, tiled=True)  24.6 us
    all_to_all x2, starting transfers between devices, body(): lax.all_to_all(by_source, 'expert', split_axis=0, concat_axis=0, tiled=True)  21.5 us
    reshape x4, local copies, waits for them, and re-layouts, body(): expert_cols.reshape(replica_count, expert_count, sub, columns)  11.2 us
    all_to_all x4, local copies, waits for them, and re-layouts, body(): lax.all_to_all(outgoing, 'expert', split_axis=0, concat_axis=0, tiled=True)  9.66 us
    dot_general x2, matrix products, body(): gate_part = jnp.dot(gathered, w_gate[0], preferred_element_type=jnp.float32)  9.32 us
  transfers between devices with their start and end apart: 13, of which 11 were waited for; matrix products, arithmetic and copies ran while one was open for 15% of the time, Pallas kernels for 0%

commit v1 on v0

--- a/solution.py
+++ b/solution.py
@@ -4,6 +4,28 @@
 from jax.sharding import PartitionSpec as P
 
 MOST_BASE = 16
+
+
+def split_up(shard, dim, length):
+    before, after = (shard.shape[:dim], shard.shape[dim + 1 :])
+    return jnp.moveaxis(shard.reshape(*before, length, -1, *after), dim, 0)
+
+
+def in_order(pieces, dim):
+    pieces = jnp.moveaxis(pieces, 0, dim)
+    shape = pieces.shape
+    return pieces.reshape(*shape[:dim], shape[dim] * shape[dim + 1], *shape[dim + 2 :])
+
+
+def pairwise_exchange(array, axis, split_dim, concat_dim):
+    length, index = (lax.axis_size(axis), lax.axis_index(axis))
+    tiles = split_up(array, split_dim, length)
+    outs = [tiles[index]]
+    for turn in range(1, length):
+        sent = tiles[index ^ turn]
+        outs.append(lax.ppermute(sent, axis, [(i, i ^ turn) for i in range(length)]))
+    tiles = jnp.stack(outs)[index ^ jnp.arange(length)]
+    return in_order(tiles, concat_dim)
 
 
 def exchange_gather(matrix, replica, replica_count):
@@ -109,7 +131,7 @@
         preferred_element_type=jnp.float32,
     ).astype(jnp.bfloat16)
     arranged = arranged.reshape(replica_count, share_rows, step_count, columns)
-    quarters = lax.all_to_all(arranged, "dp", split_axis=0, concat_axis=0, tiled=True)
+    quarters = pairwise_exchange(arranged, "dp", 0, 0)
     return quarters.transpose(1, 2, 0, 3).reshape(share_rows, step_count, model_width)
 
 

time: 303 us -> 302 us (level)
  blocking collectives: 84.3 us -> 75.5 us
  starting transfers between devices: 34.2 us -> 38.3 us
    all_to_all x1 -> x0, blocking collectives: 8.79 us -> none  [body(): lax.all_to_all(arranged, 'dp', split_axis=0, concat_axis=0, tiled=True)]
    ppermute x0 -> x3, starting transfers between devices: none -> 4.18 us  [pairwise_exchange(): lax.ppermute(sent, axis, [(i, i ^ turn) for i in range(length)])]
  transfers between devices with their start and end apart: 13 -> 16, of which waited for: 11 -> 14; matrix products, arithmetic and copies ran while one was open for 15% -> 15% of each run, Pallas kernels for 0% -> 0%
where the time goes in v1:
time: 302 us; the launch traced here: 301 us
  waiting for transfers between devices  108 us (36%)
  blocking collectives  75.5 us (25%)
  starting transfers between devices  38.3 us (13%)
  matrix products  34.4 us (11%)
  local copies, waits for them, and re-layouts  28.7 us (10%)
  between operations  14.3 us (5%)
    all_to_all x2, blocking collectives, body(): lax.all_to_all(outgoing, 'expert', split_axis=0, concat_axis=0, tiled=True)  75.5 us
    ppermute x6, waiting for transfers between devices, exchange_all(): pieces.append(lax.ppermute(block, 'dp', pairs))  46.3 us
    ppermute x3, waiting for transfers between devices, exchange_gather(): pieces.append(lax.ppermute(outgoing, 'dp', pairs))  27 us
    all_to_all x2, waiting for transfers between devices, body(): lax.all_to_all(by_source, 'expert', split_axis=0, concat_axis=0, tiled=True)  24.6 us
    all_to_all x2, starting transfers between devices, body(): lax.all_to_all(by_source, 'expert', split_axis=0, concat_axis=0, tiled=True)  21.5 us
    reshape x4, local copies, waits for them, and re-layouts, body(): expert_cols.reshape(replica_count, expert_count, sub, columns)  11.2 us
    all_to_all x4, local copies, waits for them, and re-layouts, body(): lax.all_to_all(outgoing, 'expert', split_axis=0, concat_axis=0, tiled=True)  9.65 us
    dot_general x2, matrix products, body(): gate_part = jnp.dot(gathered, w_gate[0], preferred_element_type=jnp.float32)  9.32 us
  transfers between devices with their start and end apart: 16, of which 14 were waited for; matrix products, arithmetic and copies ran while one was open for 15% of the time, Pallas kernels for 0%

profile of v1, /device:TPU:2, one launch (start us, length us, event | category | flops | bytes accessed | tf_op | source)
XLA Modules:
  0.0 300.8 jit_solution(7558365815671758302)
XLA Ops:
  6.5 3.7 %dynamic-slice_bitcast_fusion = (bf16[384,1024]{1,0:T(8,128)(2,1)}, bf16[384,1024]{1,0:T(8,128)(2,1)}, bf16[384,1024]{1,0:T(8,128)(2,1)}, bf16[384,1024]{1,0:T(8,128)(2,1)}) fusion(bf16[1,384,4096]{2,1,0:T(8,128)(2,1)} %param.17, s32[]{:T(128)S(6)} %select_n.85, s32[]{:T(128)S(6)} %select_n.81, s32[]{:T(128)S(6)} %select_n.79, s32[]{:T(128)S(6)} %select_n.83), kind=kLoop, calls=%fused_computation.41 | loop fusion | bytes 6291472 | tf_op jit(solution)/shard_map/dynamic_slice | solution.py:36
  11.9 2.9 collective-permute-start.4
  22.2 8.9 %collective-permute-done.3 = bf16[384,1024]{1,0:T(8,128)(2,1)} collective-permute-done((bf16[384,1024]{1,0:T(8,128)(2,1)}, bf16[384,1024]{1,0:T(8,128)(2,1)}, u32[]{:S(2)}, u32[]{:S(2)}) %collective-permute-start.3) | collective-permute-done | bytes 786464 | tf_op jit(solution)/shard_map/ppermute | solution.py:38
  31.2 18.0 %collective-permute-done.4 = bf16[384,1024]{1,0:T(8,128)(2,1)} collective-permute-done((bf16[384,1024]{1,0:T(8,128)(2,1)}, bf16[384,1024]{1,0:T(8,128)(2,1)}, u32[]{:S(2)}, u32[]{:S(2)}) %collective-permute-start.4) | collective-permute-done | bytes 786464 | tf_op jit(solution)/shard_map/ppermute | solution.py:38
  51.7 40.9 %all_to_all.34 = bf16[64,2,4096]{2,1,0:T(2,128)(2,1)} all-to-all(bf16[64,2,4096]{2,1,0:T(2,128)(2,1)} %all_to_all.26), channel_id=1, replica_groups=mesh['dp'=4,'expert'=64] {'expert'}, dimensions={0} | all-to-all | bytes 2097152 | tf_op jit(solution)/shard_map/all_to_all | solution.py:98
  100.1 34.5 %all_to_all.35 = bf16[64,2,4096]{2,1,0:T(2,128)(2,1)} all-to-all(bf16[64,2,4096]{2,1,0:T(2,128)(2,1)} %all_to_all.22), channel_id=1, replica_groups=mesh['dp'=4,'expert'=64] {'expert'}, dimensions={0} | all-to-all | bytes 2097152 | tf_op jit(solution)/shard_map/all_to_all | solution.py:98
  136.9 5.0 %all-gather.5.cloned.1.call-done = bf16[512,4096]{1,0:T(8,128)(2,1)} async-done(((bf16[128,4096]{1,0:T(8,128)(2,1)}), bf16[512,4096]{1,0:T(8,128)(2,1)}) %all-gather.5.cloned.1.call-update) | async-done | bytes 4194320 | tf_op jit(solution)/shard_map/all_gather | solution.py:99
  142.0 4.7 %fusion.4 = f32[512,384]{1,0:T(8,128)S(1)} fusion(bf16[512,4096]{1,0:T(8,128)(2,1)} %all-gather.5.cloned.1.call-done, bf16[1,4096,384]{2,1,0:T(8,128)(2,1)S(1)} %copy-done), kind=kOutput, calls=%fused_computation.9 | convolution fusion | flops 1610612736 | bytes 8126464 | tf_op jit(solution)/shard_map/dot_general | solution.py:100
  152.6 9.2 %collective-permute-done.8 = bf16[512,384]{1,0:T(8,128)(2,1)S(1)} collective-permute-done((bf16[512,384]{1,0:T(8,128)(2,1)S(1)}, bf16[512,384]{1,0:T(8,128)(2,1)S(1)}, u32[]{:S(2)}, u32[]{:S(2)}) %collective-permute-start.8) | collective-permute-done | bytes 393248 | tf_op jit(solution)/shard_map/ppermute | solution.py:46
  161.8 4.5 %collective-permute-done.7 = bf16[512,384]{1,0:T(8,128)(2,1)S(1)} collective-permute-done((bf16[512,384]{1,0:T(8,128)(2,1)S(1)}, bf16[512,384]{1,0:T(8,128)(2,1)S(1)}, u32[]{:S(2)}, u32[]{:S(2)}) %collective-permute-start.7) | collective-permute-done | bytes 393248 | tf_op jit(solution)/shard_map/ppermute | solution.py:46
  166.2 14.4 %collective-permute-done.6 = bf16[512,384]{1,0:T(8,128)(2,1)S(1)} collective-permute-done((bf16[512,384]{1,0:T(8,128)(2,1)S(1)}, bf16[512,384]{1,0:T(8,128)(2,1)S(1)}, u32[]{:S(2)}, u32[]{:S(2)}) %collective-permute-start.6) | collective-permute-done | bytes 393248 | tf_op jit(solution)/shard_map/ppermute | solution.py:46
  180.7 4.5 %bitcast_convert_fusion = bf16[512,1024]{1,0:T(8,128)(2,1)} fusion(bf16[1,512,384]{2,1,0:T(8,128)(2,1)S(1)} %bitcast.107, bf16[1,512,384]{2,1,0:T(8,128)(2,1)S(1)} %bitcast.109, bf16[1,512,384]{2,1,0:T(8,128)(2,1)S(1)} %bitcast.110, bf16[1,512,384]{2,1,0:T(8,128)(2,1)S(1)} %bitcast.104, bf16[1,384,1024]{2,1,0:T(8,128)(2,1)} %bitcast.16, ...), kind=kOutput, calls=%fused_computation.13 | convolution fusion | flops 1618214912 | bytes 5767168 | tf_op jit(solution)/shard_map/dot_general | solution.py:104
  187.5 3.3 %copy.47 = bf16[4,64,2,1024]{3,2,0,1:T(2,128)(2,1)} copy(bf16[4,64,2,1024]{3,2,1,0:T(2,128)(2,1)} %reshape.231) | data formatting | bytes 2097152 | tf_op jit(solution)/shard_map/reshape | solution.py:107
  190.9 10.7 %all-to-all-start.3 = ((bf16[64,4,2,1024]{3,2,1,0:T(2,128)(2,1)}), bf16[64,4,2,1024]{3,2,1,0:T(2,128)(2,1)}, u32[]{:S(2)}, u32[]{:S(2)}) async-start(bf16[64,4,2,1024]{3,2,1,0:T(2,128)(2,1)} %bitcast.93), calls=%async_computation.3 | async-start | bytes 2097152 | tf_op jit(solution)/shard_map/all_to_all | solution.py:110
  201.6 3.2 %all-gather.3.cloned.1.call-done = bf16[512,4096]{1,0:T(8,128)(2,1)} async-done(((bf16[128,4096]{1,0:T(8,128)(2,1)}), bf16[512,4096]{1,0:T(8,128)(2,1)}) %all-gather.3.cloned.1.call-update) | async-done | bytes 4194320 | tf_op jit(solution)/shard_map/all_gather | solution.py:99
  204.8 4.7 %fusion.6 = f32[512,384]{1,0:T(8,128)S(1)} fusion(bf16[512,4096]{1,0:T(8,128)(2,1)} %all-gather.3.cloned.1.call-done, bf16[1,4096,384]{2,1,0:T(8,128)(2,1)S(1)} %copy-done), kind=kOutput, calls=%fused_computation.11 | convolution fusion | flops 1610612736 | bytes 8126464 | tf_op jit(solution)/shard_map/dot_general | solution.py:100
  215.1 8.8 %collective-permute-done.2 = bf16[512,384]{1,0:T(8,128)(2,1)S(1)} collective-permute-done((bf16[512,384]{1,0:T(8,128)(2,1)S(1)}, bf16[512,384]{1,0:T(8,128)(2,1)S(1)}, u32[]{:S(2)}, u32[]{:S(2)}) %collective-permute-start.2) | collective-permute-done | bytes 393248 | tf_op jit(solution)/shard_map/ppermute | solution.py:46
  226.1 7.2 %collective-permute-done = bf16[512,384]{1,0:T(8,128)(2,1)S(1)} collective-permute-done((bf16[512,384]{1,0:T(8,128)(2,1)S(1)}, bf16[512,384]{1,0:T(8,128)(2,1)S(1)}, u32[]{:S(2)}, u32[]{:S(2)}) %collective-permute-start) | collective-permute-done | bytes 393248 | tf_op jit(solution)/shard_map/ppermute | solution.py:46
  233.2 4.4 %bitcast_convert_fusion.1 = bf16[512,1024]{1,0:T(8,128)(2,1)} fusion(bf16[1,512,384]{2,1,0:T(8,128)(2,1)S(1)} %bitcast.105, bf16[1,512,384]{2,1,0:T(8,128)(2,1)S(1)} %bitcast.106, bf16[1,512,384]{2,1,0:T(8,128)(2,1)S(1)} %bitcast.108, bf16[1,512,384]{2,1,0:T(8,128)(2,1)S(1)} %bitcast.103, bf16[1,384,1024]{2,1,0:T(8,128)(2,1)} %bitcast.16, ...), kind=kOutput, calls=%fused_computation.14 | convolution fusion | flops 1618214912 | bytes 5767168 | tf_op jit(solution)/shard_map/dot_general | solution.py:104
  239.9 3.4 %copy.48 = bf16[4,64,2,1024]{3,2,0,1:T(2,128)(2,1)} copy(bf16[4,64,2,1024]{3,2,1,0:T(2,128)(2,1)} %reshape.230) | data formatting | bytes 2097152 | tf_op jit(solution)/shard_map/reshape | solution.py:107
  243.3 10.7 %all-to-all-start.1 = ((bf16[64,4,2,1024]{3,2,1,0:T(2,128)(2,1)}), bf16[64,4,2,1024]{3,2,1,0:T(2,128)(2,1)}, u32[]{:S(2)}, u32[]{:S(2)}) async-start(bf16[64,4,2,1024]{3,2,1,0:T(2,128)(2,1)} %bitcast.92), calls=%async_computation.1 | async-start | bytes 2097152 | tf_op jit(solution)/shard_map/all_to_all | solution.py:110
  254.7 3.5 %convolution_bitcast_fusion = f32[64,1024]{1,0:T(8,128)} fusion(bf16[64,4,2,1024]{3,2,1,0:T(2,128)(2,1)} %all-to-all-done.3, s32[4,2]{1,0:T(4,128)S(1)} %iota_add_fusion, f32[64,64]{1,0:T(8,128)S(1)} %select_reduce_fusion, s32[64,64]{1,0:T(8,128)S(1)} %sub.20, pred[64,64]{1,0:T(8,128)(4,1)S(1)} %broadcast_compare_fusion), kind=kOutput, calls=%fused_computation.33 | convolution fusion | flops 201424896 | bytes 1347616 | tf_op jit(solution)/shard_map/dot_general | solution.py:117
  258.2 24.6 %all-to-all-done.1 = bf16[64,4,2,1024]{3,2,1,0:T(2,128)(2,1)} async-done(((bf16[64,4,2,1024]{3,2,1,0:T(2,128)(2,1)}), bf16[64,4,2,1024]{3,2,1,0:T(2,128)(2,1)}, u32[]{:S(2)}, u32[]{:S(2)}) %all-to-all-start.1) | async-done | bytes 1048608 | tf_op jit(solution)/shard_map/all_to_all | solution.py:110
  282.8 2.8 fusion.35
  (85 shorter events, 47.7 us)
Async XLA Ops:
  6.5 135.4 %copy-start = (bf16[1,4096,384]{2,1,0:T(8,128)(2,1)S(1)}, bf16[1,4096,384]{2,1,0:T(8,128)(2,1)}, u32[]{:S(2)}) copy-start(bf16[1,4096,384]{2,1,0:T(8,128)(2,1)} %param.15) | copy-start | bytes 9437188
  6.5 135.4 %all-gather.5.cloned.1.call-start = ((), (), s32[]{:S(2)}) async-start(), calls=%async_computation.5 | async-start | bytes 5242880 | tf_op jit(solution)/shard_map/all_gather | solution.py:99
  6.5 9.6 %copy-start.4 = (s32[16,4,8]{0,2,1:T(8,128)S(1)}, s32[16,4,8]{0,2,1:T(8,128)}, u32[]{:S(2)}) copy-start(s32[16,4,8]{0,2,1:T(8,128)} %param.10) | copy-start | bytes 6148
  6.5 10.3 %copy-start.5 = (s32[16]{0:T(128)S(1)}, s32[16]{0:T(128)}, u32[]{:S(2)}) copy-start(s32[16]{0:T(128)} %param.12) | copy-start | bytes 196
  10.3 20.9 %collective-permute-start.3 = (bf16[384,1024]{1,0:T(8,128)(2,1)}, bf16[384,1024]{1,0:T(8,128)(2,1)}, u32[]{:S(2)}, u32[]{:S(2)}) collective-permute-start(bf16[384,1024]{1,0:T(8,128)(2,1)} %get-tuple-element.16), channel_id=1, source_target_pairs={{0,64},{64,128},{128,192},{192,0},{1,65},{65,129},{129,193},{193,1... | collective-permute-start | bytes 2359304 | tf_op jit(solution)/shard_map/ppermute | solution.py:38
  11.9 37.3 %collective-permute-start.4 = (bf16[384,1024]{1,0:T(8,128)(2,1)}, bf16[384,1024]{1,0:T(8,128)(2,1)}, u32[]{:S(2)}, u32[]{:S(2)}) collective-permute-start(bf16[384,1024]{1,0:T(8,128)(2,1)} %get-tuple-element.18), channel_id=1, source_target_pairs={{0,128},{64,192},{128,0},{192,64},{1,129},{65,193},{129,1},{193,65... | collective-permute-start | bytes 2359304 | tf_op jit(solution)/shard_map/ppermute | solution.py:38
  14.8 34.4 %collective-permute-start.5 = (bf16[384,1024]{1,0:T(8,128)(2,1)}, bf16[384,1024]{1,0:T(8,128)(2,1)}, u32[]{:S(2)}, u32[]{:S(2)}) collective-permute-start(bf16[384,1024]{1,0:T(8,128)(2,1)} %get-tuple-element.15), channel_id=1, source_target_pairs={{0,192},{64,0},{128,64},{192,128},{1,193},{65,1},{129,65},{193,129... | collective-permute-start | bytes 2359304 | tf_op jit(solution)/shard_map/ppermute | solution.py:38
  95.0 109.8 %all-gather.3.cloned.1.call-start = ((), (), s32[]{:S(2)}) async-start(), calls=%async_computation.4 | async-start | bytes 5242880 | tf_op jit(solution)/shard_map/all_gather | solution.py:99
  146.6 34.1 %copy-start.1 = (bf16[384,1024]{1,0:T(8,128)(2,1)S(1)}, bf16[384,1024]{1,0:T(8,128)(2,1)}, u32[]{:S(2)}) copy-start(bf16[384,1024]{1,0:T(8,128)(2,1)} %get-tuple-element.10) | copy-start | bytes 2359300
  149.0 12.8 %collective-permute-start.8 = (bf16[512,384]{1,0:T(8,128)(2,1)S(1)}, bf16[512,384]{1,0:T(8,128)(2,1)S(1)}, u32[]{:S(2)}, u32[]{:S(2)}) collective-permute-start(bf16[512,384]{1,0:T(8,128)(2,1)S(1)} %fusion.28), channel_id=1, source_target_pairs={{0,192},{64,0},{128,64},{192,128},{1,193},{65,1},{129,65},{193,129... | collective-permute-start | bytes 1179656 | tf_op jit(solution)/shard_map/ppermute | solution.py:46
  150.2 16.1 %collective-permute-start.7 = (bf16[512,384]{1,0:T(8,128)(2,1)S(1)}, bf16[512,384]{1,0:T(8,128)(2,1)S(1)}, u32[]{:S(2)}, u32[]{:S(2)}) collective-permute-start(bf16[512,384]{1,0:T(8,128)(2,1)S(1)} %fusion.28), channel_id=1, source_target_pairs={{0,128},{64,192},{128,0},{192,64},{1,129},{65,193},{129,1},{193,65... | collective-permute-start | bytes 1179656 | tf_op jit(solution)/shard_map/ppermute | solution.py:46
  152.0 28.7 %collective-permute-start.6 = (bf16[512,384]{1,0:T(8,128)(2,1)S(1)}, bf16[512,384]{1,0:T(8,128)(2,1)S(1)}, u32[]{:S(2)}, u32[]{:S(2)}) collective-permute-start(bf16[512,384]{1,0:T(8,128)(2,1)S(1)} %fusion.28), channel_id=1, source_target_pairs={{0,64},{64,128},{128,192},{192,0},{1,65},{65,129},{129,193},{193,1... | collective-permute-start | bytes 1179656 | tf_op jit(solution)/shard_map/ppermute | solution.py:46
  190.9 52.5 %all-to-all-start.3 = ((bf16[64,4,2,1024]{3,2,1,0:T(2,128)(2,1)}), bf16[64,4,2,1024]{3,2,1,0:T(2,128)(2,1)}, u32[]{:S(2)}, u32[]{:S(2)}) async-start(bf16[64,4,2,1024]{3,2,1,0:T(2,128)(2,1)} %bitcast.93), calls=%async_computation.3 | async-start | bytes 2097152 | tf_op jit(solution)/shard_map/all_to_all | solution.py:110
  204.8 4.7 %copy-start.9 = (bf16[1,4096,384]{2,1,0:T(8,128)(2,1)S(1)}, bf16[1,4096,384]{2,1,0:T(8,128)(2,1)}, u32[]{:S(2)}) copy-start(bf16[1,4096,384]{2,1,0:T(8,128)(2,1)} %param.16) | copy-start | bytes 9437188
  209.5 23.8 %copy-start.2 = (bf16[384,1024]{1,0:T(8,128)(2,1)S(1)}, bf16[384,1024]{1,0:T(8,128)(2,1)}, u32[]{:S(2)}) copy-start(bf16[384,1024]{1,0:T(8,128)(2,1)} %get-tuple-element.10) | copy-start | bytes 2359300
  211.8 12.1 %collective-permute-start.2 = (bf16[512,384]{1,0:T(8,128)(2,1)S(1)}, bf16[512,384]{1,0:T(8,128)(2,1)S(1)}, u32[]{:S(2)}, u32[]{:S(2)}) collective-permute-start(bf16[512,384]{1,0:T(8,128)(2,1)S(1)} %fusion.31), channel_id=1, source_target_pairs={{0,192},{64,0},{128,64},{192,128},{1,193},{65,1},{129,65},{193,129... | collective-permute-start | bytes 1179656 | tf_op jit(solution)/shard_map/ppermute | solution.py:46
  212.5 13.6 %collective-permute-start.1 = (bf16[512,384]{1,0:T(8,128)(2,1)S(1)}, bf16[512,384]{1,0:T(8,128)(2,1)S(1)}, u32[]{:S(2)}, u32[]{:S(2)}) collective-permute-start(bf16[512,384]{1,0:T(8,128)(2,1)S(1)} %fusion.31), channel_id=1, source_target_pairs={{0,128},{64,192},{128,0},{192,64},{1,129},{65,193},{129,1},{193,65... | collective-permute-start | bytes 1179656 | tf_op jit(solution)/shard_map/ppermute | solution.py:46
  214.3 18.9 %collective-permute-start = (bf16[512,384]{1,0:T(8,128)(2,1)S(1)}, bf16[512,384]{1,0:T(8,128)(2,1)S(1)}, u32[]{:S(2)}, u32[]{:S(2)}) collective-permute-start(bf16[512,384]{1,0:T(8,128)(2,1)S(1)} %fusion.31), channel_id=1, source_target_pairs={{0,64},{64,128},{128,192},{192,0},{1,65},{65,129},{129,193},{193,1... | collective-permute-start | bytes 1179656 | tf_op jit(solution)/shard_map/ppermute | solution.py:46
  237.7 16.4 %copy-start.3 = (f32[16,4,8]{0,2,1:T(8,128)S(1)}, f32[16,4,8]{0,2,1:T(8,128)}, u32[]{:S(2)}) copy-start(f32[16,4,8]{0,2,1:T(8,128)} %param.11) | copy-start | bytes 6148
  237.7 16.8 %copy-start.10 = (s32[16]{0:T(128)S(1)}, s32[16]{0:T(128)}, u32[]{:S(2)}) copy-start(s32[16]{0:T(128)} %param.14) | copy-start | bytes 196
  243.3 39.5 %all-to-all-start.1 = ((bf16[64,4,2,1024]{3,2,1,0:T(2,128)(2,1)}), bf16[64,4,2,1024]{3,2,1,0:T(2,128)(2,1)}, u32[]{:S(2)}, u32[]{:S(2)}) async-start(bf16[64,4,2,1024]{3,2,1,0:T(2,128)(2,1)} %bitcast.92), calls=%async_computation.1 | async-start | bytes 2097152 | tf_op jit(solution)/shard_map/all_to_all | solution.py:110
  286.0 5.2 %collective-permute-start.11 = (bf16[1,4,4,1024]{3,2,1,0:T(4,128)(2,1)S(1)}, bf16[1,4,4,1024]{3,2,1,0:T(4,128)(2,1)S(1)}, u32[]{:S(2)}, u32[]{:S(2)}) collective-permute-start(bf16[1,4,4,1024]{3,2,1,0:T(4,128)(2,1)S(1)} %get-tuple-element.20), channel_id=1, source_target_pairs={{0,192},{64,128},{128,64},{192,0},{1,193},{65,129},{129,65},{193,1... | collective-permute-start | bytes 98312 | tf_op jit(solution)/shard_map/ppermute | solution.py:26
  287.0 5.4 %collective-permute-start.10 = (bf16[1,4,4,1024]{3,2,1,0:T(4,128)(2,1)S(1)}, bf16[1,4,4,1024]{3,2,1,0:T(4,128)(2,1)S(1)}, u32[]{:S(2)}, u32[]{:S(2)}) collective-permute-start(bf16[1,4,4,1024]{3,2,1,0:T(4,128)(2,1)S(1)} %get-tuple-element.21), channel_id=1, source_target_pairs={{0,128},{64,192},{128,0},{192,64},{1,129},{65,193},{129,1},{193,65... | collective-permute-start | bytes 98312 | tf_op jit(solution)/shard_map/ppermute | solution.py:26
  288.5 3.9 %collective-permute-start.9 = (bf16[1,4,4,1024]{3,2,1,0:T(4,128)(2,1)S(1)}, bf16[1,4,4,1024]{3,2,1,0:T(4,128)(2,1)S(1)}, u32[]{:S(2)}, u32[]{:S(2)}) collective-permute-start(bf16[1,4,4,1024]{3,2,1,0:T(4,128)(2,1)S(1)} %get-tuple-element.22), channel_id=1, source_target_pairs={{0,64},{64,0},{128,192},{192,128},{1,65},{65,1},{129,193},{193,129... | collective-permute-start | bytes 98312 | tf_op jit(solution)/shard_map/ppermute | solution.py:26
  (3 other events, 14.0 us)
Sparse Core Ops, SparseCore 0:
  95.1 46.8 all-gather.4
  143.7 60.9 all-gather.2
